TPU v7x, 256 devices: a whole 4x4x8 slice. The times are simulated.
256 devices in a mesh: seq: 32 (over z, y_lo, core), tp: 8 (over y_hi, x).
Axes of the slice: x: 4, y: 4 (y_hi: 2, y_lo: 2; y = y_hi * 2 + y_lo), z: 8, core: 2. Of those that a mesh axis runs over, the one named last changes fastest.
Arguments:
- qkv_se: bfloat16 [16384, 3, 4096], P('seq', None, 'tp'), may hold values from -6 to 6
- residual: bfloat16 [16384, 4096], P('seq', 'tp'), may hold values from -108 to 108
- taps_se: bfloat16 [256, 7], P('tp'), may hold values from -2 to 2
- skip_se: bfloat16 [4096], P('tp'), may hold values from 0.5 to 1.5
- w_out: bfloat16 [4096, 4096], P('tp', 'seq'), may hold values from -0.1875 to 0.1875
- norm_gain: bfloat16 [4096], replicated, may hold values from 0.5 to 1.5
- w_in: bfloat16 [4096, 3, 4096], P('seq', None, 'tp'), may hold values from -0.09375 to 0.09375
- taps_mr: bfloat16 [256, 128], P('tp'), may hold values from -0.5 to 0.5
- skip_mr: bfloat16 [4096], P('tp'), may hold values from 0.5 to 1.5
Outputs:
- mixed: bfloat16 [16384, 4096], P('seq', 'tp')
All inputs are finite; a program needn't handle non-finite values.
Results may differ from a plain program's by a relative error of at most 0.0085.
Values may be sent and summed in bfloat16 or wider, within the bound.
No kernel may reach another device: no remote copies, remote signals or barrier semaphores. Data moves between devices by JAX's collectives and lax.ppermute only.
A program may use at most 64 MiB of HBM per device.

v0:
```python
import jax
import jax.numpy as jnp
from jax import lax
from jax.sharding import PartitionSpec as P

GROUP = 16
SE_TAPS = 7
MR_TAPS = 128
norm_eps = 1e-05


def shifted(block, axis, distance):
    devices = range(lax.axis_size(axis))
    route = [(i - distance, i) for i in devices if i - distance in devices]
    return lax.ppermute(block, axis, route)


def toeplitz_pair(taps):
    offsets = lax.broadcasted_iota(jnp.int32, (MR_TAPS, MR_TAPS), 0) - lax.broadcasted_iota(
        jnp.int32, (MR_TAPS, MR_TAPS), 1
    )
    lag_ids = lax.broadcasted_iota(jnp.int32, (MR_TAPS, MR_TAPS, MR_TAPS), 0)
    picks = (jnp.remainder(offsets, MR_TAPS)[None] == lag_ids).astype(jnp.bfloat16)
    table = jnp.einsum("gj,jts->gts", taps, picks, preferred_element_type=jnp.float32).astype(
        jnp.bfloat16
    )
    lower = jnp.where(offsets[None] >= 0, table, jnp.zeros_like(table))
    upper = jnp.where(offsets[None] < 0, table, jnp.zeros_like(table))
    return (lower, upper)


def project_out(y_se, w_out):
    return jnp.dot(
        y_se, lax.all_gather(w_out, "seq", axis=1, tiled=True), preferred_element_type=jnp.float32
    )


def per_device(qkv_se, residual, taps_se, skip_se, w_out, norm_gain, w_in, taps_mr, skip_mr):
    row_count = qkv_se.shape[0]
    chan_width = qkv_se.shape[2]
    local_groups = chan_width // GROUP
    query_se = qkv_se[:, 0].astype(jnp.float32)
    u_se = (qkv_se[:, 1].astype(jnp.float32) * qkv_se[:, 2].astype(jnp.float32)).astype(
        jnp.bfloat16
    )
    incoming_se = shifted(u_se[row_count - (SE_TAPS - 1) :], "seq", 1)
    extended = jnp.concatenate([incoming_se, u_se], axis=0).astype(jnp.float32)
    per_channel = jnp.repeat(taps_se.astype(jnp.float32), GROUP, axis=0)
    conv_se = jnp.zeros((row_count, chan_width), jnp.float32)
    for tap_index in range(SE_TAPS):
        begin = SE_TAPS - 1 - tap_index
        conv_se = conv_se + per_channel[:, tap_index] * extended[begin : begin + row_count]
    y_se = (query_se * (conv_se + skip_se.astype(jnp.float32) * u_se.astype(jnp.float32))).astype(
        jnp.bfloat16
    )
    gain_full = norm_gain.astype(jnp.float32)
    partial_out = project_out(y_se, w_out)
    share = lax.psum_scatter(partial_out, "tp", scatter_dimension=1, tiled=True)
    stream = residual.astype(jnp.float32) + share
    squares = lax.psum(jnp.sum(stream * stream, axis=1), "tp")
    scale = lax.rsqrt(squares / (chan_width * lax.axis_size("tp")) + norm_eps)
    my_gain = lax.dynamic_slice_in_dim(gain_full, lax.axis_index("tp") * chan_width, chan_width, 0)
    normed = (stream * scale[:, None] * my_gain).astype(jnp.bfloat16)
    gathered = lax.all_gather(normed, "tp", axis=1, tiled=True)
    piece = lax.all_gather(w_in, "seq", axis=0, tiled=True)
    flat_piece = piece.reshape(piece.shape[0], 3 * chan_width)
    proj = jnp.dot(gathered, flat_piece, preferred_element_type=jnp.float32).reshape(
        row_count, 3, chan_width
    )
    query_mr = proj[:, 0]
    u_mr = (proj[:, 1] * proj[:, 2]).astype(jnp.bfloat16)
    lower, upper = toeplitz_pair(taps_mr)
    block_count = row_count // MR_TAPS
    blocks = u_mr.reshape(block_count, MR_TAPS, local_groups, GROUP)
    inside = jnp.einsum("gts,bsgc->btgc", lower, blocks, preferred_element_type=jnp.float32)
    tail_rows = shifted(blocks[block_count - 1], "seq", 1)
    earlier = jnp.concatenate([tail_rows[None], blocks[: block_count - 1]], axis=0)
    conv_mr = inside + jnp.einsum(
        "gts,bsgc->btgc", upper, earlier, preferred_element_type=jnp.float32
    )
    conv_mr = conv_mr.reshape(row_count, chan_width)
    return (query_mr * (conv_mr + skip_mr.astype(jnp.float32) * u_mr.astype(jnp.float32))).astype(
        jnp.bfloat16
    )


def solution(mesh):
    placed = (
        P("seq", None, "tp"),
        P("seq", "tp"),
        P("tp", None),
        P("tp"),
        P("tp", "seq"),
        P(),
        P("seq", None, "tp"),
        P("tp", None),
        P("tp"),
    )
    return jax.shard_map(
        per_device, mesh=mesh, in_specs=placed, out_specs=P("seq", "tp"), check_vma=False
    )
```

profile of v0, /device:TPU:105, one launch (start us, length us, event | category | flops | bytes accessed | tf_op | source)
XLA Modules:
  0.0 438.2 jit_solution(15193154201921998345)
XLA Ops:
  6.5 0.0 copy-start
  6.5 0.0 copy-start.3
  6.5 0.0 all-gather.4.cloned.1.call-start
  6.5 0.7 all-gather.4.cloned.1.call-update
  7.3 0.0 reduce-scatter.2.cloned.1.call-start
  7.3 1.3 multiply_convert_fusion.1
  8.7 5.2 %collective-permute-start = (bf16[6,512]{1,0:T(8,128)(2,1)S(1)}, bf16[6,512]{1,0:T(8,128)(2,1)S(1)}, u32[]{:S(2)}, u32[]{:S(2)}) collective-permute-start(bf16[6,512]{1,0:T(8,128)(2,1)S(1)} %slice_bitcast_fusion.1), channel_id=1, source_target_pairs={{0,8},{8,16},{16,24},{24,32},{32,40},{40,48},{48,56},{56,64},{64,7... | collective-permute-start | bytes 18440 | tf_op jit(solution)/shard_map/ppermute | solution.py:15
  13.9 0.8 broadcast_in_dim.26
  14.6 0.1 reshape.75
  14.8 1.3 fusion.51
  16.1 0.0 copy-done.3
  16.1 0.0 collective-permute-done
  16.1 0.2 maximum_convert_fusion
  16.3 65.7 %all-gather.4.cloned.1.call-done = bf16[512,4096]{1,0:T(8,128)(2,1)} async-done(((bf16[512,128]{1,0:T(8,128)(2,1)}), bf16[512,4096]{1,0:T(8,128)(2,1)}) %all-gather.4.cloned.1.call-update) | async-done | bytes 4194320 | tf_op jit(solution)/shard_map/all_gather | solution.py:34
  82.0 8.7 %fusion.22 = f32[512,4096]{1,0:T(8,128)} fusion(bf16[512,4096]{1,0:T(8,128)(2,1)} %all-gather.4.cloned.1.call-done, f32[518,512]{1,0:T(8,128)S(1)} %maximum_convert_fusion, f32[512]{0:T(512)S(1)} %convert_element_type.78, f32[512]{0:T(512)S(1)} %bitcast.74, f32[512]{0:T(512)S(1)} %bitcast.75, f32[512]{0:T(512)S(1)} %bitcast.76, f32[512]{0:T(512)S(1)} %bitcast.77, ...), kind=kOutput, calls=%fused_computation.42 | convolution fusion | flops 2152464384 | bytes 20987904 | tf_op jit(solution)/shard_map/dot_general | solution.py:33
  90.7 0.0 copy-start.2
  90.7 0.0 copy-start.1
  90.7 0.0 reduce-scatter.2.cloned.1.call-update
  90.8 0.0 copy-start.4
  90.8 0.0 all-gather.8.cloned.1.call-start
  90.8 0.9 copy-done.2
  91.7 0.9 copy.24
  92.7 0.0 all-gather.8.cloned.1.call-update
  92.7 0.0 all-gather.6.cloned.1.call-start
  92.8 0.8 dynamic-slice_convert_fusion
  93.5 115.5 %reduce-scatter.2.cloned.1.call-done = f32[512,512]{1,0:T(8,128)} async-done(((f32[512,4096]{1,0:T(8,128)}), f32[512,512]{1,0:T(8,128)}) %reduce-scatter.2.cloned.1.call-update) | async-done | bytes 1048592 | tf_op jit(solution)/shard_map/reduce_scatter | solution.py:58
  209.0 0.0 copy-done.1
  209.1 1.4 multiply_reduce_fusion
  210.5 16.9 %psum.7 = f32[512]{0:T(512)S(1)} all-reduce(f32[512]{0:T(512)S(1)} %multiply_reduce_fusion), channel_id=1, replica_groups=mesh['seq'=32,'tp'=8] {'tp'}, use_global_device_ids=true, to_apply=%region_2.0 | all-reduce | flops 512 | bytes 4096 | tf_op jit(solution)/shard_map/psum | solution.py:60
  227.4 2.3 multiply_convert_fusion
  229.7 0.0 all-gather.6.cloned.1.call-update
  229.7 0.0 copy-done.4
  229.8 0.0 copy-done
  229.8 3.3 select_bitcast_fusion
  233.1 83.3 %all-gather.8.cloned.1.call-done = bf16[4096,3,512]{0,2,1:T(8,128)(2,1)} async-done(((bf16[128,3,512]{0,2,1:T(8,128)(2,1)}), bf16[4096,3,512]{0,2,1:T(8,128)(2,1)}) %all-gather.8.cloned.1.call-update) | async-done | bytes 12582928 | tf_op jit(solution)/shard_map/all_gather | solution.py:65
  316.4 81.6 %all-gather.6.cloned.1.call-done = bf16[512,4096]{1,0:T(8,128)(2,1)} async-done(((bf16[512,512]{1,0:T(8,128)(2,1)}), bf16[512,4096]{1,0:T(8,128)(2,1)}) %all-gather.6.cloned.1.call-update) | async-done | bytes 4194320 | tf_op jit(solution)/shard_map/all_gather | solution.py:64
  398.0 10.6 %fusion = f32[512,3,512]{0,2,1:T(8,128)S(1)} fusion(bf16[4096,3,512]{0,2,1:T(8,128)(2,1)} %all-gather.8.cloned.1.call-done, bf16[512,4096]{1,0:T(8,128)(2,1)} %all-gather.6.cloned.1.call-done), kind=kOutput, calls=%fused_computation | convolution fusion | flops 6442450944 | bytes 19922944 | tf_op jit(solution)/shard_map/dot_general | solution.py:67
  408.7 0.9 fusion.9
  409.6 0.0 slice-start
  409.6 2.1 convert_element_type.84
  411.7 1.6 slice.121
  413.2 7.2 %collective-permute-start.1 = (bf16[128,32,16]{0,2,1:T(8,128)(2,1)}, bf16[128,32,16]{0,2,1:T(8,128)(2,1)}, u32[]{:S(2)}, u32[]{:S(2)}) collective-permute-start(bf16[128,32,16]{0,2,1:T(8,128)(2,1)} %bitcast.18), channel_id=1, source_target_pairs={{0,8},{8,16},{16,24},{24,32},{32,40},{40,48},{48,56},{56,64},{64,7... | collective-permute-start | bytes 393224 | tf_op jit(solution)/shard_map/ppermute | solution.py:15
  420.4 3.2 fusion.20
  423.6 0.0 slice-done
  423.6 0.9 slice.102
  424.5 1.1 copy.27
  425.6 0.0 collective-permute-done.1
  425.7 2.5 fusion.6
  428.1 0.4 copy.29
  428.6 1.0 fusion.8
  429.6 2.0 copy.30
  (7 shorter events, 0.1 us)
Async XLA Ops:
  6.5 223.3 %copy-start = (bf16[32,128]{1,0:T(8,128)(2,1)S(1)}, bf16[32,128]{1,0:T(8,128)(2,1)}, u32[]{:S(2)}) copy-start(bf16[32,128]{1,0:T(8,128)(2,1)} %param.16) | copy-start | bytes 24580
  6.5 9.6 %copy-start.3 = (bf16[512]{0:T(512)(128)(2,1)S(1)}, bf16[512]{0:T(512)(128)(2,1)}, u32[]{:S(2)}) copy-start(bf16[512]{0:T(512)(128)(2,1)} %param.12) | copy-start | bytes 3076
  6.5 75.5 %all-gather.4.cloned.1.call-start = ((), (), s32[]{:S(2)}) async-start(), calls=%async_computation.1 | async-start | bytes 4325376 | tf_op jit(solution)/shard_map/all_gather | solution.py:34
  7.3 201.8 %reduce-scatter.2.cloned.1.call-start = ((), (), s32[]{:S(2)}) async-start(), calls=%async_computation.2 | async-start | bytes 9437184 | tf_op jit(solution)/shard_map/reduce_scatter | solution.py:58
  8.7 7.5 %collective-permute-start = (bf16[6,512]{1,0:T(8,128)(2,1)S(1)}, bf16[6,512]{1,0:T(8,128)(2,1)S(1)}, u32[]{:S(2)}, u32[]{:S(2)}) collective-permute-start(bf16[6,512]{1,0:T(8,128)(2,1)S(1)} %slice_bitcast_fusion.1), channel_id=1, source_target_pairs={{0,8},{8,16},{16,24},{24,32},{32,40},{40,48},{48,56},{56,64},{64,7... | collective-permute-start | bytes 18440 | tf_op jit(solution)/shard_map/ppermute | solution.py:15
  90.7 1.0 copy-start.2
  90.7 118.3 %copy-start.1 = (bf16[512,512]{1,0:T(8,128)(2,1)S(1)}, bf16[512,512]{1,0:T(8,128)(2,1)}, u32[]{:S(2)}) copy-start(bf16[512,512]{1,0:T(8,128)(2,1)} %param.10) | copy-start | bytes 1572868
  90.8 138.9 %copy-start.4 = (bf16[512]{0:T(512)(128)(2,1)S(1)}, bf16[512]{0:T(512)(128)(2,1)}, u32[]{:S(2)}) copy-start(bf16[512]{0:T(512)(128)(2,1)} %param.17) | copy-start | bytes 3076
  90.8 225.7 %all-gather.8.cloned.1.call-start = ((), (), s32[]{:S(2)}) async-start(), calls=%async_computation.4 | async-start | bytes 12976128 | tf_op jit(solution)/shard_map/all_gather | solution.py:65
  92.7 305.3 %all-gather.6.cloned.1.call-start = ((), (), s32[]{:S(2)}) async-start(), calls=%async_computation.3 | async-start | bytes 4718592 | tf_op jit(solution)/shard_map/all_gather | solution.py:64
  409.6 14.0 %slice-start = ((bf16[512,1,512]{0,2,1:T(8,128)(2,1)}), bf16[384,1,512]{0,2,1:T(8,128)(2,1)S(1)}, s32[]{:S(2)}) async-start(bf16[512,1,512]{0,2,1:T(8,128)(2,1)} %fusion.9), calls=%async_computation.5 | async-start | bytes 786432 | tf_op jit(solution)/shard_map/slice | solution.py:77
  413.2 12.4 %collective-permute-start.1 = (bf16[128,32,16]{0,2,1:T(8,128)(2,1)}, bf16[128,32,16]{0,2,1:T(8,128)(2,1)}, u32[]{:S(2)}, u32[]{:S(2)}) collective-permute-start(bf16[128,32,16]{0,2,1:T(8,128)(2,1)} %bitcast.18), channel_id=1, source_target_pairs={{0,8},{8,16},{16,24},{24,32},{32,40},{40,48},{48,56},{56,64},{64,7... | collective-permute-start | bytes 393224 | tf_op jit(solution)/shard_map/ppermute | solution.py:15
Sparse Core Ops, SparseCore 0:
  9.1 72.8 all-gather.3
  90.9 118.1 reduce-scatter.1
  210.8 105.5 all-gather.7
  318.8 79.2 all-gather.5
where the time goes:
time: 439 us; the launch traced here: 438 us
  waiting for transfers between devices  347 us (79%)
  matrix products  28.3 us (6%)
  blocking collectives  16.9 us (4%)
  between operations  13.3 us (3%)
  starting transfers between devices  12.5 us (3%)
  local copies, waits for them, and re-layouts  10.9 us (2%)
  other arithmetic  9.38 us (2%)
    reduce_scatter x1, waiting for transfers between devices, per_device(): share = lax.psum_scatter(partial_out, 'tp', scatter_dimension=1, tiled=True)  116 us
    all_gather x1, waiting for transfers between devices, per_device(): piece = lax.all_gather(w_in, 'seq', axis=0, tiled=True)  83.3 us
    all_gather x1, waiting for transfers between devices, per_device(): gathered = lax.all_gather(normed, 'tp', axis=1, tiled=True)  81.6 us
    all_gather x1, waiting for transfers between devices, project_out(): lax.all_gather(w_out, 'seq', axis=1, tiled=True)  65.7 us
    psum x1, blocking collectives, per_device(): squares = lax.psum(jnp.sum(stream * stream, axis=1), 'tp')  16.9 us
    ppermute x2, starting transfers between devices, shifted(): return lax.ppermute(block, axis, route)  12.4 us
    dot_general x1, matrix products, per_device(): jnp.dot(gathered, flat_piece, preferred_element_type=jnp.float32)  10.6 us
  transfers between devices with their start and end apart: 6, of which 4 were waited for; matrix products, arithmetic and copies ran while one was open for 4% of the time, Pallas kernels for 0%

commit v1 on v0

--- a/solution.py
+++ b/solution.py
@@ -61,7 +61,9 @@
     scale = lax.rsqrt(squares / (chan_width * lax.axis_size("tp")) + norm_eps)
     my_gain = lax.dynamic_slice_in_dim(gain_full, lax.axis_index("tp") * chan_width, chan_width, 0)
     normed = (stream * scale[:, None] * my_gain).astype(jnp.bfloat16)
-    gathered = lax.all_gather(normed, "tp", axis=1, tiled=True)
+    gathered = jnp.concatenate(
+        lax.all_to_all(jnp.stack([normed] * lax.axis_size("tp")), "tp", 0, 0), axis=1
+    )
     piece = lax.all_gather(w_in, "seq", axis=0, tiled=True)
     flat_piece = piece.reshape(piece.shape[0], 3 * chan_width)
     proj = jnp.dot(gathered, flat_piece, preferred_element_type=jnp.float32).reshape(

time: 439 us -> 398 us (0.907); the launches traced: 438 us -> 390 us
  waiting for transfers between devices: 347 us -> 281 us
  local copies, waits for them, and re-layouts: 10.9 us -> 27 us
    all_gather x1 -> x0, waiting for transfers between devices: 81.6 us -> none  [per_device(): gathered = lax.all_gather(normed, 'tp', axis=1, tiled=True)]
    all_to_all x0 -> x1, waiting for transfers between devices: none -> 47.7 us  [per_device(): lax.all_to_all(jnp.stack([normed] * lax.axis_size('tp')), 'tp', 0, 0)]
    all_gather x1, waiting for transfers between devices: 83.3 us -> 52.2 us  [per_device(): piece = lax.all_gather(w_in, 'seq', axis=0, tiled=True)]
    reshape x0 -> x2, local copies, waits for them, and re-layouts: none -> 13.9 us  [per_device(): jnp.concatenate(lax.all_to_all(jnp.stack([normed] * lax.axis_size('tp')),...]
    all_to_all x0 -> x1, starting transfers between devices: none -> 4.71 us  [per_device(): lax.all_to_all(jnp.stack([normed] * lax.axis_size('tp')), 'tp', 0, 0)]
  transfers between devices with their start and end apart: 6 -> 6, of which waited for: 4 -> 4; matrix products, arithmetic and copies ran while one was open for 4% -> 9% of each run, Pallas kernels for 0% -> 0%
where the time goes in v1:
time: 398 us; the launch traced here: 390 us
  waiting for transfers between devices  281 us (71%)
  matrix products  28.3 us (7%)
  local copies, waits for them, and re-layouts  27 us (7%)
  blocking collectives  16.9 us (4%)
  starting transfers between devices  14.4 us (4%)
  between operations  13.3 us (3%)
  other arithmetic  9.27 us (2%)
    reduce_scatter x1, waiting for transfers between devices, per_device(): share = lax.psum_scatter(partial_out, 'tp', scatter_dimension=1, tiled=True)  116 us
    all_gather x1, waiting for transfers between devices, project_out(): lax.all_gather(w_out, 'seq', axis=1, tiled=True)  65.1 us
    all_gather x1, waiting for transfers between devices, per_device(): piece = lax.all_gather(w_in, 'seq', axis=0, tiled=True)  52.2 us
    all_to_all x1, waiting for transfers between devices, per_device(): lax.all_to_all(jnp.stack([normed] * lax.axis_size('tp')), 'tp', 0, 0)  47.7 us
    psum x1, blocking collectives, per_device(): squares = lax.psum(jnp.sum(stream * stream, axis=1), 'tp')  16.9 us
    reshape x2, local copies, waits for them, and re-layouts, per_device(): jnp.concatenate(lax.all_to_all(jnp.stack([normed] * lax.axis_size('tp')),...  13.9 us
    dot_general x1, matrix products, per_device(): jnp.dot(gathered, flat_piece, preferred_element_type=jnp.float32)  10.6 us
    ppermute x2, starting transfers between devices, shifted(): return lax.ppermute(block, axis, route)  9.56 us
  transfers between devices with their start and end apart: 6, of which 4 were waited for; matrix products, arithmetic and copies ran while one was open for 9% of the time, Pallas kernels for 0%

profile of v1, /device:TPU:105, one launch (start us, length us, event | category | flops | bytes accessed | tf_op | source)
XLA Modules:
  0.0 390.4 jit_solution(17602491862667941647)
XLA Ops:
  6.5 0.0 copy-start
  6.5 0.0 all-gather.3.cloned.1.call-start
  6.5 0.7 all-gather.3.cloned.1.call-update
  7.3 0.0 reduce-scatter.2.cloned.1.call-start
  7.3 1.3 multiply_convert_fusion.1
  8.7 5.2 %collective-permute-start = (bf16[6,512]{1,0:T(8,128)(2,1)S(1)}, bf16[6,512]{1,0:T(8,128)(2,1)S(1)}, u32[]{:S(2)}, u32[]{:S(2)}) collective-permute-start(bf16[6,512]{1,0:T(8,128)(2,1)S(1)} %slice_bitcast_fusion.1), channel_id=1, source_target_pairs={{0,8},{8,16},{16,24},{24,32},{32,40},{40,48},{48,56},{56,64},{64,7... | collective-permute-start | bytes 18440 | tf_op jit(solution)/shard_map/ppermute | solution.py:15
  13.9 0.8 broadcast_in_dim.26
  14.6 0.1 reshape.83
  14.8 1.3 fusion.51
  16.1 0.7 convert_element_type.78
  16.8 0.0 collective-permute-done
  16.8 0.2 maximum_convert_fusion
  17.0 65.1 %all-gather.3.cloned.1.call-done = bf16[512,4096]{1,0:T(8,128)(2,1)} async-done(((bf16[512,128]{1,0:T(8,128)(2,1)}), bf16[512,4096]{1,0:T(8,128)(2,1)}) %all-gather.3.cloned.1.call-update) | async-done | bytes 4194320 | tf_op jit(solution)/shard_map/all_gather | solution.py:34
  82.0 8.7 %fusion.21 = f32[512,4096]{1,0:T(8,128)} fusion(bf16[512,4096]{1,0:T(8,128)(2,1)} %all-gather.3.cloned.1.call-done, f32[518,512]{1,0:T(8,128)S(1)} %maximum_convert_fusion, f32[512]{0:T(512)S(1)} %convert_element_type.78, f32[512]{0:T(512)S(1)} %bitcast.73, f32[512]{0:T(512)S(1)} %bitcast.74, f32[512]{0:T(512)S(1)} %bitcast.75, f32[512]{0:T(512)S(1)} %bitcast.76, ...), kind=kOutput, calls=%fused_computation.41 | convolution fusion | flops 2152464384 | bytes 20987904 | tf_op jit(solution)/shard_map/dot_general | solution.py:33
  90.7 0.0 copy-start.2
  90.7 0.0 copy-start.1
  90.7 0.0 reduce-scatter.2.cloned.1.call-update
  90.8 0.0 all-gather.5.cloned.1.call-start
  90.8 0.9 copy-done.2
  91.7 0.9 copy.32
  92.7 0.0 all-gather.5.cloned.1.call-update
  92.7 0.8 dynamic-slice_convert_fusion
  93.4 115.6 %reduce-scatter.2.cloned.1.call-done = f32[512,512]{1,0:T(8,128)} async-done(((f32[512,4096]{1,0:T(8,128)}), f32[512,512]{1,0:T(8,128)}) %reduce-scatter.2.cloned.1.call-update) | async-done | bytes 1048592 | tf_op jit(solution)/shard_map/reduce_scatter | solution.py:58
  209.1 0.0 copy-done.1
  209.1 1.4 multiply_reduce_fusion
  210.5 16.9 %psum.7 = f32[512]{0:T(512)S(1)} all-reduce(f32[512]{0:T(512)S(1)} %multiply_reduce_fusion), channel_id=1, replica_groups=mesh['seq'=32,'tp'=8] {'tp'}, use_global_device_ids=true, to_apply=%region_2.0 | all-reduce | flops 512 | bytes 4096 | tf_op jit(solution)/shard_map/psum | solution.py:60
  227.4 1.5 multiply_convert_fusion
  228.9 2.3 stack.2
  231.2 0.0 copy-start.3
  231.2 4.7 %all-to-all-start = ((bf16[8,512,512]{2,1,0:T(8,128)(2,1)}), bf16[8,512,512]{2,1,0:T(8,128)(2,1)}, u32[]{:S(2)}, u32[]{:S(2)}) async-start(bf16[8,512,512]{2,1,0:T(8,128)(2,1)} %stack.2), calls=%async_computation.1 | async-start | bytes 8388608 | tf_op jit(solution)/shard_map/all_to_all | solution.py:65
  235.9 0.0 copy-done.3
  236.0 0.0 copy-done
  236.0 3.3 select_bitcast_fusion
  239.4 47.7 %all-to-all-done = bf16[8,512,512]{2,1,0:T(8,128)(2,1)} async-done(((bf16[8,512,512]{2,1,0:T(8,128)(2,1)}), bf16[8,512,512]{2,1,0:T(8,128)(2,1)}, u32[]{:S(2)}, u32[]{:S(2)}) %all-to-all-start) | async-done | bytes 4194336 | tf_op jit(solution)/shard_map/all_to_all | solution.py:65
  287.0 6.5 %copy.31 = bf16[512,8,512]{2,1,0:T(8,128)(2,1)} copy(bf16[512,8,512]{2,0,1:T(8,128)(2,1)} %bitcast.10) | data formatting | bytes 8388608 | tf_op jit(solution)/shard_map/reshape | solution.py:64
  293.5 7.4 %reshape.90 = bf16[512,4096,1]{1,0,2:T(8,128)(2,1)} reshape(bf16[512,8,512]{2,1,0:T(8,128)(2,1)} %copy.31) | data formatting | bytes 8388608 | tf_op jit(solution)/shard_map/reshape | solution.py:64
  300.9 52.2 %all-gather.5.cloned.1.call-done = bf16[4096,3,512]{0,2,1:T(8,128)(2,1)} async-done(((bf16[128,3,512]{0,2,1:T(8,128)(2,1)}), bf16[4096,3,512]{0,2,1:T(8,128)(2,1)}) %all-gather.5.cloned.1.call-update) | async-done | bytes 12582928 | tf_op jit(solution)/shard_map/all_gather | solution.py:67
  353.1 10.6 %fusion = f32[512,3,512]{0,2,1:T(8,128)S(1)} fusion(bf16[512,4096,1]{1,0,2:T(8,128)(2,1)} %reshape.90, bf16[4096,3,512]{0,2,1:T(8,128)(2,1)} %all-gather.5.cloned.1.call-done), kind=kOutput, calls=%fused_computation | convolution fusion | flops 6442450944 | bytes 19922944 | tf_op jit(solution)/shard_map/dot_general | solution.py:69
  363.7 0.9 fusion.8
  364.6 0.0 slice-start
  364.6 2.1 convert_element_type.84
  366.7 1.6 slice.121
  368.2 4.4 %collective-permute-start.1 = (bf16[128,32,16]{0,2,1:T(8,128)(2,1)}, bf16[128,32,16]{0,2,1:T(8,128)(2,1)}, u32[]{:S(2)}, u32[]{:S(2)}) collective-permute-start(bf16[128,32,16]{0,2,1:T(8,128)(2,1)} %bitcast.18), channel_id=1, source_target_pairs={{0,8},{8,16},{16,24},{24,32},{32,40},{40,48},{48,56},{56,64},{64,7... | collective-permute-start | bytes 393224 | tf_op jit(solution)/shard_map/ppermute | solution.py:15
  372.6 3.2 fusion.19
  375.8 0.0 slice-done
  375.8 0.9 slice.102
  376.7 1.1 copy.35
  377.8 0.0 collective-permute-done.1
  377.8 2.5 fusion.5
  380.3 0.4 copy.37
  380.8 1.0 fusion.7
  381.8 2.0 copy.38
  (6 shorter events, 0.1 us)
Async XLA Ops:
  6.5 229.5 %copy-start = (bf16[32,128]{1,0:T(8,128)(2,1)S(1)}, bf16[32,128]{1,0:T(8,128)(2,1)}, u32[]{:S(2)}) copy-start(bf16[32,128]{1,0:T(8,128)(2,1)} %param.16) | copy-start | bytes 24580
  6.5 75.5 %all-gather.3.cloned.1.call-start = ((), (), s32[]{:S(2)}) async-start(), calls=%async_computation.2 | async-start | bytes 4325376 | tf_op jit(solution)/shard_map/all_gather | solution.py:34
  7.3 201.8 %reduce-scatter.2.cloned.1.call-start = ((), (), s32[]{:S(2)}) async-start(), calls=%async_computation.3 | async-start | bytes 9437184 | tf_op jit(solution)/shard_map/reduce_scatter | solution.py:58
  8.7 8.1 %collective-permute-start = (bf16[6,512]{1,0:T(8,128)(2,1)S(1)}, bf16[6,512]{1,0:T(8,128)(2,1)S(1)}, u32[]{:S(2)}, u32[]{:S(2)}) collective-permute-start(bf16[6,512]{1,0:T(8,128)(2,1)S(1)} %slice_bitcast_fusion.1), channel_id=1, source_target_pairs={{0,8},{8,16},{16,24},{24,32},{32,40},{40,48},{48,56},{56,64},{64,7... | collective-permute-start | bytes 18440 | tf_op jit(solution)/shard_map/ppermute | solution.py:15
  90.7 1.0 copy-start.2
  90.7 118.3 %copy-start.1 = (bf16[512,512]{1,0:T(8,128)(2,1)S(1)}, bf16[512,512]{1,0:T(8,128)(2,1)}, u32[]{:S(2)}) copy-start(bf16[512,512]{1,0:T(8,128)(2,1)} %param.10) | copy-start | bytes 1572868
  90.8 262.3 %all-gather.5.cloned.1.call-start = ((), (), s32[]{:S(2)}) async-start(), calls=%async_computation.4 | async-start | bytes 12976128 | tf_op jit(solution)/shard_map/all_gather | solution.py:67
  231.2 4.7 %copy-start.3 = (bf16[512]{0:T(512)(128)(2,1)S(1)}, bf16[512]{0:T(512)(128)(2,1)}, u32[]{:S(2)}) copy-start(bf16[512]{0:T(512)(128)(2,1)} %param.17) | copy-start | bytes 3076
  231.2 55.8 %all-to-all-start = ((bf16[8,512,512]{2,1,0:T(8,128)(2,1)}), bf16[8,512,512]{2,1,0:T(8,128)(2,1)}, u32[]{:S(2)}, u32[]{:S(2)}) async-start(bf16[8,512,512]{2,1,0:T(8,128)(2,1)} %stack.2), calls=%async_computation.1 | async-start | bytes 8388608 | tf_op jit(solution)/shard_map/all_to_all | solution.py:65
  364.6 11.2 %slice-start = ((bf16[512,1,512]{0,2,1:T(8,128)(2,1)}), bf16[384,1,512]{0,2,1:T(8,128)(2,1)S(1)}, s32[]{:S(2)}) async-start(bf16[512,1,512]{0,2,1:T(8,128)(2,1)} %fusion.8), calls=%async_computation.5 | async-start | bytes 786432 | tf_op jit(solution)/shard_map/slice | solution.py:79
  368.2 9.6 %collective-permute-start.1 = (bf16[128,32,16]{0,2,1:T(8,128)(2,1)}, bf16[128,32,16]{0,2,1:T(8,128)(2,1)}, u32[]{:S(2)}, u32[]{:S(2)}) collective-permute-start(bf16[128,32,16]{0,2,1:T(8,128)(2,1)} %bitcast.18), channel_id=1, source_target_pairs={{0,8},{8,16},{16,24},{24,32},{32,40},{40,48},{48,56},{56,64},{64,7... | collective-permute-start | bytes 393224 | tf_op jit(solution)/shard_map/ppermute | solution.py:15
Sparse Core Ops, SparseCore 0:
  9.1 72.8 all-gather.2
  90.9 118.1 reduce-scatter.1
  210.8 142.1 all-gather.4
